TPU v7x, 32 devices: a whole 2x2x4 slice. The times are simulated.
32 devices in a mesh: clips: 2 (over y), patch: 4 (over z), span: 2 (over x), chan: 2 (over core).
Axes of the slice: x: 2, y: 2, z: 4, core: 2. Of those that a mesh axis runs over, the one named last changes fastest.
Arguments:
- latent_tiles: bfloat16 [4, 256, 4, 384], P(('clips', 'span'), 'patch'), parts along dimension 0, may hold values from -12 to 12
- route: int32 [4, 256], P(('clips', 'span')), parts along dimension 0, may hold values from 0 to 255, as said below
- w_query: bfloat16 [384, 384], replicated, may hold values from -0.5 to 4.6
- w_keyval: bfloat16 [384, 768], replicated, may hold values from -0.5 to 4.6
- conv_weight: bfloat16 [3, 3, 3, 384, 384], P(None, None, None, None, 'chan'), may hold values from -0.0625 to 0.0625
Outputs:
- decoded: bfloat16 [8, 8, 64, 384], P(('clips', 'span'), 'patch', None, 'chan'), parts along dimension 0
There are 2 independent parts, one for each index of `clips`. A program takes and returns all parts, laid end to end along the dimension named above; an argument that names none is the same for every part. Nothing has to cross between parts.
Inputs may be any that keep to these rules, and one draw needn't show every extreme that they name: `route`: each span's row is a permutation of 0 .. 255. The 64 tiles of positions j * 64 to (j + 1) * 64 - 1 go to at most 32 per owner, and in every span some such group sends exactly 32 to one owner.
All inputs are finite; a program needn't handle non-finite values.
Results may differ from a plain program's by a relative error of at most 0.0065.
Values may be sent and summed in bfloat16 or wider, within the bound.
No kernel may reach another device: no remote copies, remote signals or barrier semaphores. Data moves between devices by JAX's collectives and lax.ppermute only.
A program may use at most 64 MiB of HBM per device.

v0:
```python
import math
import jax
import jax.numpy as jnp
from jax import lax
from jax.sharding import PartitionSpec as P

C = 384
W = 64
RD = 2
FD = 2
epsilon = 1e-06


def scaled_rms(values):
    wide = values.astype(jnp.float32)
    return wide / jnp.sqrt(jnp.mean(wide * wide, axis=-1, keepdims=True) + epsilon)


def attend(queries, key_rows, value_rows):
    scale = 1.0 / math.sqrt(queries.shape[-1])
    scores = (
        jnp.einsum("fqc,fkc->fqk", queries, key_rows, preferred_element_type=jnp.float32) * scale
    )
    largest = jnp.max(scores, axis=-1, keepdims=True)
    powers = jnp.exp(scores - largest)
    totals = jnp.sum(powers, axis=-1, keepdims=True)
    weights = powers.astype(jnp.bfloat16)
    summed = jnp.einsum("fqk,fkc->fqc", weights, value_rows, preferred_element_type=jnp.float32)
    return summed / totals


def spatial_conv(frames, kernel):
    return lax.conv_general_dilated(
        frames,
        kernel,
        (1, 1),
        ((0, 0), (1, 1)),
        dimension_numbers=("NHWC", "HWIO", "NHWC"),
        preferred_element_type=jnp.float32,
    )


def local(latent_tiles, route, w_query, w_keyval, conv_weight):
    patch_count = lax.axis_size("patch")
    patch_index = lax.axis_index("patch")
    chan_count = lax.axis_size("chan")
    chan_index = lax.axis_index("chan")
    span_count = lax.axis_size("span")
    table = route[0]
    block = latent_tiles.shape[1]
    share = block // chan_count
    own_share = lax.dynamic_slice_in_dim(latent_tiles, chan_index * share, share, 1)
    every_tile = lax.all_gather(own_share, ("patch", "chan"), axis=1, tiled=True)[0]
    tile_total = every_tile.shape[0]
    rows = patch_count * RD
    slots = jnp.arange(tile_total, dtype=jnp.int32)
    one_hot = (slots[:, None] == table[None, :]).astype(jnp.bfloat16)
    placed = jnp.dot(
        one_hot, every_tile.reshape(tile_total, -1), preferred_element_type=jnp.float32
    ).astype(jnp.bfloat16)
    placed = placed.reshape(patch_count, FD, RD, W, C)
    whole = placed.transpose(1, 0, 2, 3, 4).reshape(FD, rows, W, C)
    normed_all = scaled_rms(whole).astype(jnp.bfloat16)
    padded = jnp.pad(whole, ((0, 0), (1, 1), (0, 0), (0, 0)))
    features = lax.dynamic_slice_in_dim(padded, patch_index * RD, RD + 2, 1)
    normed = scaled_rms(features).astype(jnp.bfloat16)
    ext_cells = (RD + 2) * W
    queries = jnp.einsum(
        "fnc,cd->fnd", normed.reshape(FD, ext_cells, C), w_query, preferred_element_type=jnp.float32
    ).astype(jnp.bfloat16)
    keyvals = jnp.einsum(
        "fnc,cd->fnd",
        normed_all.reshape(FD, rows * W, C),
        w_keyval,
        preferred_element_type=jnp.float32,
    ).astype(jnp.bfloat16)
    attended = attend(queries, keyvals[..., :C], keyvals[..., C:])
    mixed = (features.astype(jnp.float32) + attended.reshape(FD, RD + 2, W, C)).astype(jnp.bfloat16)
    row_ids = patch_index * RD - 1 + jnp.arange(RD + 2)
    inside = ((row_ids >= 0) & (row_ids < rows))[None, :, None, None]
    activated = jnp.where(inside, jax.nn.silu(scaled_rms(mixed)), 0.0).astype(jnp.bfloat16)
    by_first = spatial_conv(activated, conv_weight[0])
    by_middle = spatial_conv(activated[1:], conv_weight[1])
    to_next = jnp.concatenate([by_first[:1] + by_middle, by_first[1:]]).astype(jnp.bfloat16)
    pairs = [(i, i + 1) for i in range(span_count - 1)]
    from_prev = lax.ppermute(to_next, "span", pairs)
    by_last = spatial_conv(activated, conv_weight[2])
    own_middle = spatial_conv(activated[:1], conv_weight[1])
    own_sum = jnp.concatenate([by_last[:1], own_middle + by_last[1:]])
    out_width = conv_weight.shape[-1]
    own_rows = mixed[:, 1 : RD + 1]
    own_channels = lax.dynamic_slice_in_dim(own_rows, chan_index * out_width, out_width, 3)
    return (own_channels.astype(jnp.float32) + own_sum + from_prev.astype(jnp.float32)).astype(
        jnp.bfloat16
    )


def solution(mesh):
    placed = (
        P(("clips", "span"), "patch", None, None),
        P(("clips", "span"), None),
        P(),
        P(),
        P(None, None, None, None, "chan"),
    )
    return jax.shard_map(
        local,
        mesh=mesh,
        in_specs=placed,
        out_specs=P(("clips", "span"), "patch", None, "chan"),
        check_vma=False,
    )
```

profile of v0, /device:TPU:0, one launch (start us, length us, event | category | flops | bytes accessed | tf_op | source)
XLA Modules:
  0.0 41.3 jit_solution(17983313363802852854)
XLA Ops:
  0.0 1.0 %constant_dynamic-slice_fusion = bf16[1,32,4,384]{3,2,0,1:T(4,128)(2,1)S(1)} fusion(bf16[1,64,4,384]{3,2,0,1:T(4,128)(2,1)} %bitcast.114, s32[]{:T(128)S(6)} %select_n.13), kind=kLoop, calls=%fused_computation.87 | loop fusion | bytes 196612 | tf_op jit(solution)/shard_map/dynamic_slice | solution.py:52
  1.0 17.2 %all_gather.3 = bf16[1,256,4,384]{3,2,0,1:T(4,128)(2,1)S(1)} all-gather(bf16[1,32,4,384]{3,2,0,1:T(4,128)(2,1)S(1)} %constant_dynamic-slice_fusion), channel_id=1, replica_groups=mesh['clips'=2,'patch'=4,'span'=2,'chan'=2] {'patch','chan'}, dimensions={1}, use_global_device_ids=true | all-gather | bytes 884736 | tf_op jit(solution)/shard_map/all_gather | solution.py:53
  18.4 0.4 convolution_convert_fusion
  18.7 0.5 %reshape.60 = bf16[4,2,2,64,384]{4,3,2,1,0:T(8,128)(2,1)S(1)} reshape(bf16[256,1536]{1,0:T(8,128)(2,1)S(1)} %convolution_convert_fusion) | data formatting | bytes 1572864 | tf_op jit(solution)/shard_map/reshape | solution.py:61
  19.2 0.2 multiply_reduce_fusion
  19.4 1.4 %fusion.72 = (bf16[4,2,2,64,384]{4,3,2,0,1:T(8,128)(2,1)S(1)}, f32[2,4,2,64,384]{4,3,2,1,0:T(8,128)}) fusion(bf16[4,2,2,64,384]{4,3,2,1,0:T(8,128)(2,1)S(1)} %reshape.60), kind=kLoop, calls=%fused_computation.94 | loop fusion | flops 393216 | bytes 3145728 | tf_op jit(solution)/shard_map/reshape | solution.py:61
  21.0 0.2 fusion.28
  21.1 0.2 fusion.29
  21.3 0.9 %copy-done.1 = f32[2,4,2,64,384]{4,3,2,1,0:T(8,128)S(1)} copy-done((f32[2,4,2,64,384]{4,3,2,1,0:T(8,128)S(1)}, f32[2,4,2,64,384]{4,3,2,1,0:T(8,128)}, u32[]{:S(2)}) %copy-start.1) | copy-done | bytes 1572888
  22.2 0.2 fusion
  22.5 2.1 %convolution_convert_fusion.1 = bf16[2,512,768]{2,1,0:T(8,128)(2,1)} fusion(bf16[2,512,384]{2,1,0:T(8,128)(2,1)S(1)} %fusion, bf16[384,768]{1,0:T(8,128)(2,1)S(1)} %copy-done), kind=kOutput, calls=%fused_computation.2 | convolution fusion | flops 604766208 | bytes 2949120 | tf_op jit(solution)/shard_map/fnc,cd->fnd/dot_general | solution.py:71
  24.6 1.9 %fusion.74 = (f32[2,256]{1,0:T(2,128)S(1)}, f32[2,256,512]{2,1,0:T(8,128)S(1)}) fusion(bf16[2,512,768]{2,1,0:T(8,128)(2,1)} %convolution_convert_fusion.1, bf16[2,256,384]{2,1,0:T(8,128)(2,1)S(1)} %bitcast.112, bf16[384,384]{1,0:T(8,128)(2,1)S(1)} %copy-done.4), kind=kOutput, calls=%fused_computation.96 | convolution fusion | flops 353041920 | bytes 2525184 | tf_op jit(solution)/shard_map/fqc,fkc->fqk/dot_general | solution.py:22
  26.5 0.3 fusion.25
  26.9 1.6 %convolution_divide_fusion = f32[2,256,384]{2,1,0:T(8,128)S(1)} fusion(bf16[2,512,768]{2,1,0:T(8,128)(2,1)} %convolution_convert_fusion.1, f32[2,256,512]{2,1,0:T(8,128)S(1)} %get-tuple-element.14, f32[2,256]{1,0:T(2,128)S(1)} %get-tuple-element.13, f32[2,256]{1,0:T(2,128)S(1)} %fusion.25), kind=kOutput, calls=%fused_computation.17 | convolution fusion | flops 202047488 | bytes 2625536 | tf_op jit(solution)/shard_map/fqk,fkc->fqc/dot_general | solution.py:28
  28.5 0.2 fusion.27
  28.8 0.3 fusion.81
  29.1 0.3 select_convert_fusion
  29.5 0.4 copy.116
  29.9 0.2 copy.118
  30.2 0.7 %copy-done.3 = bf16[3,3,3,384,192]{3,4,2,1,0:T(8,128)(2,1)S(1)} copy-done((bf16[3,3,3,384,192]{3,4,2,1,0:T(8,128)(2,1)S(1)}, bf16[3,3,3,384,192]{3,4,2,1,0:T(8,128)(2,1)}, u32[]{:S(2)}) %copy-start.3) | copy-done | bytes 3981336
  30.9 0.6 %fusion.22 = f32[2,8,9,192]{3,1,2,0:T(8,128)S(1)} fusion(bf16[3,3,3,384,192]{3,4,2,1,0:T(8,128)(2,1)S(1)} %copy-done.3, bf16[4,1,7,2,384]{4,2,3,0,1:T(8,128)(2,1)S(1)} %slice.72, bf16[4,1,8,9,384]{4,2,3,0,1:T(8,128)(2,1)S(1)} %copy.105, pred[8,9]{0,1:T(8,128)(4,1)S(1)} %copy-done.5), kind=kOutput, calls=%fused_computation.27 | convolution fusion | flops 191941632 | bytes 1710080 | tf_op jit(solution)/shard_map/conv_general_dilated | solution.py:33
  31.6 0.3 pad.5.clone
  32.0 0.5 %fusion.34 = bf16[4,2,8,11,384]{4,1,3,2,0:T(2,128)(2,1)S(1)} fusion(bf16[4,2,7,2,384]{4,1,3,2,0:T(2,128)(2,1)S(1)} %slice.62, bf16[4,2,8,9,384]{4,1,3,2,0:T(2,128)(2,1)S(1)} %bitcast.101), kind=kLoop, calls=%fused_computation.43 | loop fusion | flops 1622016 | bytes 1069056 | tf_op jit(solution)/shard_map/conv_general_dilated | solution.py:33
  32.5 0.7 %fusion.77 = (bf16[2,16,9,192]{3,1,2,0:T(8,128)(2,1)S(1)}, f32[2,16,9,192]{3,1,2,0:T(8,128)S(1)}) fusion(bf16[3,3,3,384,192]{3,4,2,1,0:T(8,128)(2,1)S(1)} %copy-done.3, bf16[4,2,8,11,384]{4,1,3,2,0:T(2,128)(2,1)S(1)} %fusion.34, pred[16,9]{0,1:T(8,128)(4,1)S(1)} %copy-done.6), kind=kOutput, calls=%fused_computation.97 | convolution fusion | flops 382316544 | bytes 2201600 | tf_op jit(solution)/shard_map/conv_general_dilated | solution.py:33
  33.5 0.2 copy.101
  33.8 3.4 %collective-permute-start = (bf16[2,2,64,192]{3,2,1,0:T(8,128)(2,1)S(1)}, bf16[2,2,64,192]{3,2,1,0:T(8,128)(2,1)S(1)}, u32[]{:S(2)}, u32[]{:S(2)}) collective-permute-start(bf16[2,2,64,192]{3,2,1,0:T(8,128)(2,1)S(1)} %pad_maximum_fusion), channel_id=1, source_target_pairs={{0,2},{1,3},{4,6},{5,7},{8,10},{9,11},{12,14},{13,15},{16,18},{17,... | collective-permute-start | bytes 294920 | tf_op jit(solution)/shard_map/ppermute | solution.py:86
  37.3 0.7 %fusion.11 = f32[2,16,9,192]{3,1,2,0:T(8,128)S(1)} fusion(bf16[3,3,3,384,192]{3,4,2,1,0:T(8,128)(2,1)S(1)} %copy-done.3, bf16[4,2,8,11,384]{4,1,3,2,0:T(2,128)(2,1)S(1)} %fusion.34, pred[16,9]{0,1:T(8,128)(4,1)S(1)} %copy-done.6), kind=kOutput, calls=%fused_computation.22 | convolution fusion | flops 382261248 | bytes 2091008 | tf_op jit(solution)/shard_map/conv_general_dilated | solution.py:33
  38.0 0.2 copy.117
  38.3 0.6 %fusion.19 = f32[2,8,9,192]{3,1,2,0:T(8,128)S(1)} fusion(bf16[3,3,3,384,192]{3,4,2,1,0:T(8,128)(2,1)S(1)} %copy-done.3, bf16[4,1,7,2,384]{4,2,3,0,1:T(8,128)(2,1)S(1)} %slice.66, bf16[4,1,8,9,384]{4,2,3,0,1:T(8,128)(2,1)S(1)} %copy.98, pred[8,9]{0,1:T(8,128)(4,1)S(1)} %copy-done.5), kind=kOutput, calls=%fused_computation.26 | convolution fusion | flops 191941632 | bytes 1710080 | tf_op jit(solution)/shard_map/conv_general_dilated | solution.py:33
  39.0 0.2 copy.94
  39.4 1.1 %collective-permute-done = bf16[2,2,64,192]{3,2,1,0:T(8,128)(2,1)S(1)} collective-permute-done((bf16[2,2,64,192]{3,2,1,0:T(8,128)(2,1)S(1)}, bf16[2,2,64,192]{3,2,1,0:T(8,128)(2,1)S(1)}, u32[]{:S(2)}, u32[]{:S(2)}) %collective-permute-start) | collective-permute-done | bytes 98336 | tf_op jit(solution)/shard_map/ppermute | solution.py:86
  40.5 0.8 %fusion.58 = bf16[2,2,64,192]{3,2,1,0:T(8,128)(2,1)} fusion(f32[1,2,64,192]{3,2,1,0:T(8,128)S(1)} %get-tuple-element.12, f32[1,2,64,192]{3,2,1,0:T(8,128)S(1)} %get-tuple-element.11, bf16[2,2,64,192]{3,2,1,0:T(8,128)(2,1)S(1)} %collective-permute-done, bf16[2,2,64,384]{3,2,1,0:T(8,128)(2,1)S(1)} %slice.61, s32[]{:T(128)S(6)} %select_n.15), kind=kLoop, calls=%fused_computation.65 | loop fusion | flops 294912 | bytes 491524 | tf_op jit(solution)/shard_map/convert_element_type | solution.py:93
  (43 shorter events, 1.2 us)
Async XLA Ops:
  0.0 22.5 %copy-start = (bf16[384,768]{1,0:T(8,128)(2,1)S(1)}, bf16[384,768]{1,0:T(8,128)(2,1)}, u32[]{:S(2)}) copy-start(bf16[384,768]{1,0:T(8,128)(2,1)} %param.8) | copy-start | bytes 1769476
  0.0 18.4 %copy-start.2 = (s32[1,256]{1,0:T(1,128)S(1)}, s32[1,256]{1,0:T(1,128)}, u32[]{:S(2)}) copy-start(s32[1,256]{1,0:T(1,128)} %param.6) | copy-start | bytes 3076
  20.8 1.4 %copy-start.1 = (f32[2,4,2,64,384]{4,3,2,1,0:T(8,128)S(1)}, f32[2,4,2,64,384]{4,3,2,1,0:T(8,128)}, u32[]{:S(2)}) copy-start(f32[2,4,2,64,384]{4,3,2,1,0:T(8,128)} %get-tuple-element.8) | copy-start | bytes 4718596
  22.5 2.1 %copy-start.4 = (bf16[384,384]{1,0:T(8,128)(2,1)S(1)}, bf16[384,384]{1,0:T(8,128)(2,1)}, u32[]{:S(2)}) copy-start(bf16[384,384]{1,0:T(8,128)(2,1)} %param.7) | copy-start | bytes 884740
  28.8 2.1 %copy-start.3 = (bf16[3,3,3,384,192]{3,4,2,1,0:T(8,128)(2,1)S(1)}, bf16[3,3,3,384,192]{3,4,2,1,0:T(8,128)(2,1)}, u32[]{:S(2)}) copy-start(bf16[3,3,3,384,192]{3,4,2,1,0:T(8,128)(2,1)} %param.9) | copy-start | bytes 11943940
  29.4 1.4 %copy-start.5 = (pred[8,9]{0,1:T(8,128)(4,1)S(1)}, pred[8,9]{0,1:T(8,128)(4,1)}, u32[]{:S(2)}) copy-start(pred[8,9]{0,1:T(8,128)(4,1)} %constant.70) | copy-start | bytes 220
  31.5 1.0 %copy-start.6 = (pred[16,9]{0,1:T(8,128)(4,1)S(1)}, pred[16,9]{0,1:T(8,128)(4,1)}, u32[]{:S(2)}) copy-start(pred[16,9]{0,1:T(8,128)(4,1)} %constant.69) | copy-start | bytes 436
  33.8 6.7 %collective-permute-start = (bf16[2,2,64,192]{3,2,1,0:T(8,128)(2,1)S(1)}, bf16[2,2,64,192]{3,2,1,0:T(8,128)(2,1)S(1)}, u32[]{:S(2)}, u32[]{:S(2)}) collective-permute-start(bf16[2,2,64,192]{3,2,1,0:T(8,128)(2,1)S(1)} %pad_maximum_fusion), channel_id=1, source_target_pairs={{0,2},{1,3},{4,6},{5,7},{8,10},{9,11},{12,14},{13,15},{16,18},{17,... | collective-permute-start | bytes 294920 | tf_op jit(solution)/shard_map/ppermute | solution.py:86
where the time goes:
time: 41.5 us; the launch traced here: 41.3 us
  blocking collectives  17.2 us (41%)
  matrix products  8.7 us (21%)
  local copies, waits for them, and re-layouts  5.65 us (14%)
  other arithmetic  4.7 us (11%)
  starting transfers between devices  3.41 us (8%)
  waiting for transfers between devices  1.14 us (3%)
  between operations  0.43 us (1%)
    all_gather x1, blocking collectives, local(): lax.all_gather(own_share, ('patch', 'chan'), axis=1, tiled=True)[0]  17.2 us
    ppermute x1, starting transfers between devices, local(): from_prev = lax.ppermute(to_next, 'span', pairs)  3.41 us
    conv_general_dilated x4, matrix products, spatial_conv(): lax.conv_general_dilated(frames, kernel, (1, 1), ((0, 0), (1, 1)), dimens...  2.61 us
    unnamed x21, local copies, waits for them, and re-layouts  2.5 us
    dot_general x1, matrix products, local(): jnp.einsum('fnc,cd->fnd', normed_all.reshape(FD, rows * W, C), w_keyval,...  2.13 us
    dot_general x1, matrix products, attend(): jnp.einsum('fqc,fkc->fqk', queries, key_rows, preferred_element_type=jnp....  1.93 us
    dot_general x1, matrix products, attend(): jnp.einsum('fqk,fkc->fqc', weights, value_rows, preferred_element_type=jn...  1.65 us
    reshape x1, other arithmetic, local(): placed = placed.reshape(patch_count, FD, RD, W, C)  1.39 us
  transfers between devices with their start and end apart: 1, of which 1 were waited for; matrix products, arithmetic and copies ran while one was open for 5% of the time, Pallas kernels for 0%

commit v1 on v0

--- a/solution.py
+++ b/solution.py
@@ -1,14 +1,45 @@
+import functools
 import math
 import jax
 import jax.numpy as jnp
 from jax import lax
 from jax.sharding import PartitionSpec as P
+from jax.lax import axis_index, axis_size, ppermute
 
 C = 384
 W = 64
 RD = 2
 FD = 2
 epsilon = 1e-06
+
+
+def treat_the_sources_all(shard_in, dimension_no):
+    part_now = list(shard_in.shape[1:])
+    part_now[dimension_no] *= shard_in.shape[0]
+    return jnp.moveaxis(shard_in, 0, dimension_no).reshape(part_now)
+
+
+def start_entries_all(message, row_axis, in_dim):
+    sides = axis_size(row_axis)
+    line_up = [(no, (no + 1) % sides) for no in range(sides)]
+    series = [(kk, dev_j) for dev_j, kk in line_up]
+    new, x_now = ([], [])
+    for rr in tuple(range(sides - 1)):
+        if rr % 2 == 0:
+            t1 = ppermute(new[-1] if new else message, row_axis, perm=line_up)
+            new.append(t1)
+        else:
+            y = ppermute(x_now[-1] if x_now else message, row_axis, series)
+            x_now.append(y)
+    f_next = jnp.stack([*new[::-1], message, *x_now])
+    all_values = axis_index(row_axis)
+    upper = len(new)
+    reached = all_values - upper
+    f_next = f_next[(jnp.arange(sides) - reached) % sides]
+    return treat_the_sources_all(f_next, in_dim)
+
+
+step_on_the_floor = functools.partial(start_entries_all, row_axis=("patch", "chan"), in_dim=1)
 
 
 def scaled_rms(values):
@@ -50,7 +81,7 @@
     block = latent_tiles.shape[1]
     share = block // chan_count
     own_share = lax.dynamic_slice_in_dim(latent_tiles, chan_index * share, share, 1)
-    every_tile = lax.all_gather(own_share, ("patch", "chan"), axis=1, tiled=True)[0]
+    every_tile = step_on_the_floor(own_share)[0]
     tile_total = every_tile.shape[0]
     rows = patch_count * RD
     slots = jnp.arange(tile_total, dtype=jnp.int32)

time: 41.5 us -> 53.1 us (1.28)
  blocking collectives: 17.2 us -> 0 us
  waiting for transfers between devices: 1.14 us -> 15.1 us
  starting transfers between devices: 3.41 us -> 15.7 us
  local copies, waits for them, and re-layouts: 5.65 us -> 8 us
    all_gather x1 -> x0, blocking collectives: 17.2 us -> none  [local(): lax.all_gather(own_share, ('patch', 'chan'), axis=1, tiled=True)[0]]
    ppermute x0 -> x7, waiting for transfers between devices: none -> 12.7 us  [the longest x4 12.6 us: start_entries_all(): t1 = ppermute(new[-1] if new else message, row_axis, perm=line_up)]
    ppermute x0 -> x7, starting transfers between devices: none -> 11.8 us  [the longest x3 11.3 us: start_entries_all(): y = ppermute(x_now[-1] if x_now else message, row_axis, series)]
    gather x0 -> x1, local copies, waits for them, and re-layouts: none -> 1.29 us  [start_entries_all(): f_next = f_next[(jnp.arange(sides) - reached) % sides]]
    ppermute x1, waiting for transfers between devices: 1.14 us -> 2.43 us  [local(): from_prev = lax.ppermute(to_next, 'span', pairs)]
    unnamed x21 -> x28, local copies, waits for them, and re-layouts: 2.5 us -> 3.51 us
    ppermute x1, starting transfers between devices: 3.41 us -> 3.96 us  [local(): from_prev = lax.ppermute(to_next, 'span', pairs)]
  transfers between devices with their start and end apart: 1 -> 8, of which waited for: 1 -> 5; matrix products, arithmetic and copies ran while one was open for 5% -> 2% of each run, Pallas kernels for 0% -> 0%
where the time goes in v1:
time: 53.1 us; the launch traced here: 52.8 us
  starting transfers between devices  15.7 us (30%)
  waiting for transfers between devices  15.1 us (28%)
  matrix products  8.71 us (16%)
  local copies, waits for them, and re-layouts  8 us (15%)
  other arithmetic  4.75 us (9%)
    ppermute x4, waiting for transfers between devices, start_entries_all(): t1 = ppermute(new[-1] if new else message, row_axis, perm=line_up)  12.6 us
    ppermute x3, starting transfers between devices, start_entries_all(): y = ppermute(x_now[-1] if x_now else message, row_axis, series)  11.3 us
    ppermute x1, starting transfers between devices, local(): from_prev = lax.ppermute(to_next, 'span', pairs)  3.96 us
    unnamed x28, local copies, waits for them, and re-layouts  3.51 us
    conv_general_dilated x4, matrix products, spatial_conv(): lax.conv_general_dilated(frames, kernel, (1, 1), ((0, 0), (1, 1)), dimens...  2.61 us
    ppermute x1, waiting for transfers between devices, local(): from_prev = lax.ppermute(to_next, 'span', pairs)  2.43 us
    dot_general x1, matrix products, local(): jnp.einsum('fnc,cd->fnd', normed_all.reshape(FD, rows * W, C), w_keyval,...  2.13 us
    dot_general x1, matrix products, attend(): jnp.einsum('fqc,fkc->fqk', queries, key_rows, preferred_element_type=jnp....  1.93 us
  transfers between devices with their start and end apart: 8, of which 5 were waited for; matrix products, arithmetic and copies ran while one was open for 2% of the time, Pallas kernels for 0%

profile of v1, /device:TPU:0, one launch (start us, length us, event | category | flops | bytes accessed | tf_op | source)
XLA Modules:
  0.0 52.8 jit_solution(6447855888058519807)
XLA Ops:
  0.0 1.0 %constant_dynamic-slice_fusion = bf16[1,32,4,384]{3,2,1,0:T(4,128)(2,1)S(1)} fusion(bf16[1,64,4,384]{3,2,1,0:T(4,128)(2,1)} %param.5, s32[]{:T(128)S(6)} %select_n.37), kind=kLoop, calls=%fused_computation.101 | loop fusion | bytes 196612 | tf_op jit(solution)/shard_map/dynamic_slice | solution.py:83
  1.0 0.5 collective-permute-start
  1.5 4.1 %collective-permute-start.4 = (bf16[1,32,4,384]{3,2,1,0:T(4,128)(2,1)S(1)}, bf16[1,32,4,384]{3,2,1,0:T(4,128)(2,1)S(1)}, u32[]{:S(2)}, u32[]{:S(2)}) collective-permute-start(bf16[1,32,4,384]{3,2,1,0:T(4,128)(2,1)S(1)} %constant_dynamic-slice_fusion), channel_id=1, source_target_pairs={{1,0},{4,1},{5,4},{8,5},{9,8},{12,9},{13,12},{0,13},{3,2},{6,3},{7... | collective-permute-start | bytes 294920 | tf_op jit(solution)/shard_map/ppermute | solution.py:32
  5.6 2.3 %collective-permute-done = bf16[1,32,4,384]{3,2,1,0:T(4,128)(2,1)S(1)} collective-permute-done((bf16[1,32,4,384]{3,2,1,0:T(4,128)(2,1)S(1)}, bf16[1,32,4,384]{3,2,1,0:T(4,128)(2,1)S(1)}, u32[]{:S(2)}, u32[]{:S(2)}) %collective-permute-start) | collective-permute-done | bytes 98336 | tf_op jit(solution)/shard_map/ppermute | solution.py:29
  7.9 5.8 %collective-permute-done.1 = bf16[1,32,4,384]{3,2,1,0:T(4,128)(2,1)S(1)} collective-permute-done((bf16[1,32,4,384]{3,2,1,0:T(4,128)(2,1)S(1)}, bf16[1,32,4,384]{3,2,1,0:T(4,128)(2,1)S(1)}, u32[]{:S(2)}, u32[]{:S(2)}) %collective-permute-start.1) | collective-permute-done | bytes 98336 | tf_op jit(solution)/shard_map/ppermute | solution.py:29
  13.8 3.6 %collective-permute-start.5 = (bf16[1,32,4,384]{3,2,1,0:T(4,128)(2,1)S(1)}, bf16[1,32,4,384]{3,2,1,0:T(4,128)(2,1)S(1)}, u32[]{:S(2)}, u32[]{:S(2)}) collective-permute-start(bf16[1,32,4,384]{3,2,1,0:T(4,128)(2,1)S(1)} %collective-permute-done.4), channel_id=1, source_target_pairs={{1,0},{4,1},{5,4},{8,5},{9,8},{12,9},{13,12},{0,13},{3,2},{6,3},{7... | collective-permute-start | bytes 294920 | tf_op jit(solution)/shard_map/ppermute | solution.py:32
  17.3 2.3 %collective-permute-done.2 = bf16[1,32,4,384]{3,2,1,0:T(4,128)(2,1)S(1)} collective-permute-done((bf16[1,32,4,384]{3,2,1,0:T(4,128)(2,1)S(1)}, bf16[1,32,4,384]{3,2,1,0:T(4,128)(2,1)S(1)}, u32[]{:S(2)}, u32[]{:S(2)}) %collective-permute-start.2) | collective-permute-done | bytes 98336 | tf_op jit(solution)/shard_map/ppermute | solution.py:29
  19.7 3.6 %collective-permute-start.6 = (bf16[1,32,4,384]{3,2,1,0:T(4,128)(2,1)S(1)}, bf16[1,32,4,384]{3,2,1,0:T(4,128)(2,1)S(1)}, u32[]{:S(2)}, u32[]{:S(2)}) collective-permute-start(bf16[1,32,4,384]{3,2,1,0:T(4,128)(2,1)S(1)} %collective-permute-done.5), channel_id=1, source_target_pairs={{1,0},{4,1},{5,4},{8,5},{9,8},{12,9},{13,12},{0,13},{3,2},{6,3},{7... | collective-permute-start | bytes 294920 | tf_op jit(solution)/shard_map/ppermute | solution.py:32
  23.3 2.2 %collective-permute-done.3 = bf16[1,32,4,384]{3,2,1,0:T(4,128)(2,1)S(1)} collective-permute-done((bf16[1,32,4,384]{3,2,1,0:T(4,128)(2,1)S(1)}, bf16[1,32,4,384]{3,2,1,0:T(4,128)(2,1)S(1)}, u32[]{:S(2)}, u32[]{:S(2)}) %collective-permute-start.3) | collective-permute-done | bytes 98336 | tf_op jit(solution)/shard_map/ppermute | solution.py:29
  25.7 0.9 %bitcast_dynamic-update-slice_fusion.3 = bf16[8,1,32,4,384]{4,3,2,1,0:T(4,128)(2,1)S(1)} fusion(bf16[8,1,32,4,384]{4,3,2,1,0:T(4,128)(2,1)S(1)} %bitcast_dynamic-update-slice_fusion.4, bf16[1,64,4,384]{3,2,1,0:T(4,128)(2,1)} %param.5, s32[]{:T(128)S(6)} %select_n.37), kind=kLoop, calls=%fused_computation.85 | loop fusion | bytes 196612
  26.8 1.3 %gather_fusion = bf16[8,32,4,384]{3,2,1,0:T(4,128)(2,1)S(1)} fusion(bf16[8,32,4,384]{3,2,1,0:T(4,128)(2,1)S(1)} %bitcast.122, s32[1024]{0:T(1024)S(1)} %pad_clamp_fusion), kind=kCustom, calls=%fused_computation | custom fusion | bytes 1572896 | tf_op jit(solution)/shard_map/gather | solution.py:38
  28.3 0.4 convolution_convert_fusion
  28.6 0.5 reshape.109
  29.3 1.4 %fusion.74 = (bf16[4,2,2,64,384]{4,3,2,0,1:T(8,128)(2,1)S(1)}, f32[2,4,2,64,384]{4,3,2,1,0:T(8,128)}) fusion(bf16[4,2,2,64,384]{4,3,2,1,0:T(8,128)(2,1)S(1)} %reshape.109), kind=kLoop, calls=%fused_computation.110 | loop fusion | flops 393216 | bytes 3145728 | tf_op jit(solution)/shard_map/reshape | solution.py:92
  31.2 0.9 %copy-done.1 = f32[2,4,2,64,384]{4,3,2,1,0:T(8,128)S(1)} copy-done((f32[2,4,2,64,384]{4,3,2,1,0:T(8,128)S(1)}, f32[2,4,2,64,384]{4,3,2,1,0:T(8,128)}, u32[]{:S(2)}) %copy-start.1) | copy-done | bytes 1572888
  32.4 2.1 %convolution_convert_fusion.1 = bf16[2,512,768]{2,1,0:T(8,128)(2,1)} fusion(bf16[2,512,384]{2,1,0:T(8,128)(2,1)S(1)} %fusion, bf16[384,768]{1,0:T(8,128)(2,1)S(1)} %copy-done), kind=kOutput, calls=%fused_computation.3 | convolution fusion | flops 604766208 | bytes 2949120 | tf_op jit(solution)/shard_map/fnc,cd->fnd/dot_general | solution.py:102
  34.5 1.9 %fusion.76 = (f32[2,256]{1,0:T(2,128)S(1)}, f32[2,256,512]{2,1,0:T(8,128)S(1)}) fusion(bf16[2,512,768]{2,1,0:T(8,128)(2,1)} %convolution_convert_fusion.1, bf16[2,256,384]{2,1,0:T(8,128)(2,1)S(1)} %bitcast.130, bf16[384,384]{1,0:T(8,128)(2,1)S(1)} %copy-done.4), kind=kOutput, calls=%fused_computation.112 | convolution fusion | flops 353041920 | bytes 2525184 | tf_op jit(solution)/shard_map/fqc,fkc->fqk/dot_general | solution.py:53
  36.5 0.3 fusion.25
  36.8 1.7 %convolution_divide_fusion = f32[2,256,384]{2,1,0:T(8,128)S(1)} fusion(bf16[2,512,768]{2,1,0:T(8,128)(2,1)} %convolution_convert_fusion.1, f32[2,256,512]{2,1,0:T(8,128)S(1)} %get-tuple-element.14, f32[2,256]{1,0:T(2,128)S(1)} %get-tuple-element.13, f32[2,256]{1,0:T(2,128)S(1)} %fusion.25), kind=kOutput, calls=%fused_computation.18 | convolution fusion | flops 202047488 | bytes 2625536 | tf_op jit(solution)/shard_map/fqk,fkc->fqc/dot_general | solution.py:59
  38.7 0.3 fusion.83
  39.0 0.3 select_convert_fusion
  39.4 0.4 copy.113
  39.8 0.3 pad.5.clone
  40.2 0.5 fusion.34
  40.8 0.7 %fusion.11 = f32[2,16,9,192]{3,1,2,0:T(8,128)S(1)} fusion(bf16[3,3,3,384,192]{3,4,2,1,0:T(8,128)(2,1)S(1)} %copy-done.3, bf16[4,2,8,11,384]{4,1,3,2,0:T(2,128)(2,1)S(1)} %fusion.34, pred[16,9]{0,1:T(8,128)(4,1)S(1)} %copy-done.6), kind=kOutput, calls=%fused_computation.23 | convolution fusion | flops 382261248 | bytes 2091008 | tf_op jit(solution)/shard_map/conv_general_dilated | solution.py:64
  41.6 0.7 %fusion.79 = (bf16[2,16,9,192]{3,1,2,0:T(8,128)(2,1)S(1)}, f32[2,16,9,192]{3,1,2,0:T(8,128)S(1)}) fusion(bf16[3,3,3,384,192]{3,4,2,1,0:T(8,128)(2,1)S(1)} %copy-done.3, bf16[4,2,8,11,384]{4,1,3,2,0:T(2,128)(2,1)S(1)} %fusion.34, pred[16,9]{0,1:T(8,128)(4,1)S(1)} %copy-done.6), kind=kOutput, calls=%fused_computation.113 | convolution fusion | flops 382316544 | bytes 2201600 | tf_op jit(solution)/shard_map/conv_general_dilated | solution.py:64
  42.7 0.3 copy-done.5
  43.0 0.6 %fusion.22 = f32[2,8,9,192]{3,1,2,0:T(8,128)S(1)} fusion(bf16[3,3,3,384,192]{3,4,2,1,0:T(8,128)(2,1)S(1)} %copy-done.3, bf16[4,1,7,2,384]{4,2,3,0,1:T(8,128)(2,1)S(1)} %slice.74, bf16[4,1,8,9,384]{4,2,3,0,1:T(8,128)(2,1)S(1)} %copy.102, pred[8,9]{0,1:T(8,128)(4,1)S(1)} %copy-done.5), kind=kOutput, calls=%fused_computation.28 | convolution fusion | flops 191941632 | bytes 1710080 | tf_op jit(solution)/shard_map/conv_general_dilated | solution.py:64
  44.0 0.6 %fusion.19 = f32[2,8,9,192]{3,1,2,0:T(8,128)S(1)} fusion(bf16[3,3,3,384,192]{3,4,2,1,0:T(8,128)(2,1)S(1)} %copy-done.3, bf16[4,1,7,2,384]{4,2,3,0,1:T(8,128)(2,1)S(1)} %slice.68, bf16[4,1,8,9,384]{4,2,3,0,1:T(8,128)(2,1)S(1)} %copy.95, pred[8,9]{0,1:T(8,128)(4,1)S(1)} %copy-done.5), kind=kOutput, calls=%fused_computation.27 | convolution fusion | flops 191941632 | bytes 1710080 | tf_op jit(solution)/shard_map/conv_general_dilated | solution.py:64
  45.6 4.0 %collective-permute-start.7 = (bf16[2,2,64,192]{3,2,1,0:T(8,128)(2,1)S(1)}, bf16[2,2,64,192]{3,2,1,0:T(8,128)(2,1)S(1)}, u32[]{:S(2)}, u32[]{:S(2)}) collective-permute-start(bf16[2,2,64,192]{3,2,1,0:T(8,128)(2,1)S(1)} %pad_maximum_fusion), channel_id=1, source_target_pairs={{0,2},{1,3},{4,6},{5,7},{8,10},{9,11},{12,14},{13,15},{16,18},{17,... | collective-permute-start | bytes 294920 | tf_op jit(solution)/shard_map/ppermute | solution.py:117
  49.6 2.4 %collective-permute-done.7 = bf16[2,2,64,192]{3,2,1,0:T(8,128)(2,1)S(1)} collective-permute-done((bf16[2,2,64,192]{3,2,1,0:T(8,128)(2,1)S(1)}, bf16[2,2,64,192]{3,2,1,0:T(8,128)(2,1)S(1)}, u32[]{:S(2)}, u32[]{:S(2)}) %collective-permute-start.7) | collective-permute-done | bytes 98336 | tf_op jit(solution)/shard_map/ppermute | solution.py:117
  52.0 0.8 %fusion.58 = bf16[2,2,64,192]{3,2,1,0:T(8,128)(2,1)} fusion(f32[1,2,64,192]{3,2,1,0:T(8,128)S(1)} %get-tuple-element.12, f32[1,2,64,192]{3,2,1,0:T(8,128)S(1)} %get-tuple-element.11, bf16[2,2,64,192]{3,2,1,0:T(8,128)(2,1)S(1)} %collective-permute-done.7, bf16[2,2,64,384]{3,2,1,0:T(8,128)(2,1)S(1)} %slice.63, s32[]{:T(128)S(6)} %select_n.41), kind=kLoop, calls=%fused_computation.66 | loop fusion | flops 294912 | bytes 491524 | tf_op jit(solution)/shard_map/convert_element_type | solution.py:124
  (67 shorter events, 3.4 us)
Async XLA Ops:
  0.0 32.4 %copy-start = (bf16[384,768]{1,0:T(8,128)(2,1)S(1)}, bf16[384,768]{1,0:T(8,128)(2,1)}, u32[]{:S(2)}) copy-start(bf16[384,768]{1,0:T(8,128)(2,1)} %param.8) | copy-start | bytes 1769476
  1.0 6.9 %collective-permute-start = (bf16[1,32,4,384]{3,2,1,0:T(4,128)(2,1)S(1)}, bf16[1,32,4,384]{3,2,1,0:T(4,128)(2,1)S(1)}, u32[]{:S(2)}, u32[]{:S(2)}) collective-permute-start(bf16[1,32,4,384]{3,2,1,0:T(4,128)(2,1)S(1)} %constant_dynamic-slice_fusion), channel_id=1, source_target_pairs={{0,1},{1,4},{4,5},{5,8},{8,9},{9,12},{12,13},{13,0},{2,3},{3,6},{6... | collective-permute-start | bytes 294920 | tf_op jit(solution)/shard_map/ppermute | solution.py:29
  1.5 12.2 %collective-permute-start.4 = (bf16[1,32,4,384]{3,2,1,0:T(4,128)(2,1)S(1)}, bf16[1,32,4,384]{3,2,1,0:T(4,128)(2,1)S(1)}, u32[]{:S(2)}, u32[]{:S(2)}) collective-permute-start(bf16[1,32,4,384]{3,2,1,0:T(4,128)(2,1)S(1)} %constant_dynamic-slice_fusion), channel_id=1, source_target_pairs={{1,0},{4,1},{5,4},{8,5},{9,8},{12,9},{13,12},{0,13},{3,2},{6,3},{7... | collective-permute-start | bytes 294920 | tf_op jit(solution)/shard_map/ppermute | solution.py:32
  7.9 5.8 %collective-permute-start.1 = (bf16[1,32,4,384]{3,2,1,0:T(4,128)(2,1)S(1)}, bf16[1,32,4,384]{3,2,1,0:T(4,128)(2,1)S(1)}, u32[]{:S(2)}, u32[]{:S(2)}) collective-permute-start(bf16[1,32,4,384]{3,2,1,0:T(4,128)(2,1)S(1)} %collective-permute-done), channel_id=1, source_target_pairs={{0,1},{1,4},{4,5},{5,8},{8,9},{9,12},{12,13},{13,0},{2,3},{3,6},{6... | collective-permute-start | bytes 294920 | tf_op jit(solution)/shard_map/ppermute | solution.py:29
  13.7 5.9 %collective-permute-start.2 = (bf16[1,32,4,384]{3,2,1,0:T(4,128)(2,1)S(1)}, bf16[1,32,4,384]{3,2,1,0:T(4,128)(2,1)S(1)}, u32[]{:S(2)}, u32[]{:S(2)}) collective-permute-start(bf16[1,32,4,384]{3,2,1,0:T(4,128)(2,1)S(1)} %collective-permute-done.1), channel_id=1, source_target_pairs={{0,1},{1,4},{4,5},{5,8},{8,9},{9,12},{12,13},{13,0},{2,3},{3,6},{6... | collective-permute-start | bytes 294920 | tf_op jit(solution)/shard_map/ppermute | solution.py:29
  13.8 5.9 %collective-permute-start.5 = (bf16[1,32,4,384]{3,2,1,0:T(4,128)(2,1)S(1)}, bf16[1,32,4,384]{3,2,1,0:T(4,128)(2,1)S(1)}, u32[]{:S(2)}, u32[]{:S(2)}) collective-permute-start(bf16[1,32,4,384]{3,2,1,0:T(4,128)(2,1)S(1)} %collective-permute-done.4), channel_id=1, source_target_pairs={{1,0},{4,1},{5,4},{8,5},{9,8},{12,9},{13,12},{0,13},{3,2},{6,3},{7... | collective-permute-start | bytes 294920 | tf_op jit(solution)/shard_map/ppermute | solution.py:32
  19.6 5.8 %collective-permute-start.3 = (bf16[1,32,4,384]{3,2,1,0:T(4,128)(2,1)S(1)}, bf16[1,32,4,384]{3,2,1,0:T(4,128)(2,1)S(1)}, u32[]{:S(2)}, u32[]{:S(2)}) collective-permute-start(bf16[1,32,4,384]{3,2,1,0:T(4,128)(2,1)S(1)} %collective-permute-done.2), channel_id=1, source_target_pairs={{0,1},{1,4},{4,5},{5,8},{8,9},{9,12},{12,13},{13,0},{2,3},{3,6},{6... | collective-permute-start | bytes 294920 | tf_op jit(solution)/shard_map/ppermute | solution.py:29
  19.7 7.1 %collective-permute-start.6 = (bf16[1,32,4,384]{3,2,1,0:T(4,128)(2,1)S(1)}, bf16[1,32,4,384]{3,2,1,0:T(4,128)(2,1)S(1)}, u32[]{:S(2)}, u32[]{:S(2)}) collective-permute-start(bf16[1,32,4,384]{3,2,1,0:T(4,128)(2,1)S(1)} %collective-permute-done.5), channel_id=1, source_target_pairs={{1,0},{4,1},{5,4},{8,5},{9,8},{12,9},{13,12},{0,13},{3,2},{6,3},{7... | collective-permute-start | bytes 294920 | tf_op jit(solution)/shard_map/ppermute | solution.py:32
  26.8 1.4 %copy-start.2 = (s32[1,256]{1,0:T(1,128)S(1)}, s32[1,256]{1,0:T(1,128)}, u32[]{:S(2)}) copy-start(s32[1,256]{1,0:T(1,128)} %param.6) | copy-start | bytes 3076
  30.8 1.4 %copy-start.1 = (f32[2,4,2,64,384]{4,3,2,1,0:T(8,128)S(1)}, f32[2,4,2,64,384]{4,3,2,1,0:T(8,128)}, u32[]{:S(2)}) copy-start(f32[2,4,2,64,384]{4,3,2,1,0:T(8,128)} %get-tuple-element.8) | copy-start | bytes 4718596
  32.4 2.1 %copy-start.4 = (bf16[384,384]{1,0:T(8,128)(2,1)S(1)}, bf16[384,384]{1,0:T(8,128)(2,1)}, u32[]{:S(2)}) copy-start(bf16[384,384]{1,0:T(8,128)(2,1)} %param.7) | copy-start | bytes 884740
  38.7 2.1 %copy-start.3 = (bf16[3,3,3,384,192]{3,4,2,1,0:T(8,128)(2,1)S(1)}, bf16[3,3,3,384,192]{3,4,2,1,0:T(8,128)(2,1)}, u32[]{:S(2)}) copy-start(bf16[3,3,3,384,192]{3,4,2,1,0:T(8,128)(2,1)} %param.9) | copy-start | bytes 11943940
  39.4 1.4 %copy-start.6 = (pred[16,9]{0,1:T(8,128)(4,1)S(1)}, pred[16,9]{0,1:T(8,128)(4,1)}, u32[]{:S(2)}) copy-start(pred[16,9]{0,1:T(8,128)(4,1)} %constant.87) | copy-start | bytes 436
  42.3 0.7 %copy-start.5 = (pred[8,9]{0,1:T(8,128)(4,1)S(1)}, pred[8,9]{0,1:T(8,128)(4,1)}, u32[]{:S(2)}) copy-start(pred[8,9]{0,1:T(8,128)(4,1)} %constant.88) | copy-start | bytes 220
  45.6 6.5 %collective-permute-start.7 = (bf16[2,2,64,192]{3,2,1,0:T(8,128)(2,1)S(1)}, bf16[2,2,64,192]{3,2,1,0:T(8,128)(2,1)S(1)}, u32[]{:S(2)}, u32[]{:S(2)}) collective-permute-start(bf16[2,2,64,192]{3,2,1,0:T(8,128)(2,1)S(1)} %pad_maximum_fusion), channel_id=1, source_target_pairs={{0,2},{1,3},{4,6},{5,7},{8,10},{9,11},{12,14},{13,15},{16,18},{17,... | collective-permute-start | bytes 294920 | tf_op jit(solution)/shard_map/ppermute | solution.py:117
